TPU v7x, 256 devices: a whole 4x4x8 slice. The times are simulated.
256 devices in a mesh: section: 2 (over core), expert: 32 (over x, z), dp: 4 (over y).
Axes of the slice: x: 4, y: 4, z: 8, core: 2. Of those that a mesh axis runs over, the one named last changes fastest.
Arguments:
- tokens: bfloat16 [2, 16384, 1024], P(None, ('expert', 'dp')), may hold values from -6 to 6
- cotangent: bfloat16 [2, 16384, 1024], P(None, ('expert', 'dp')), may hold values from -6 to 6
- routes: int32 [2, 2, 16384, 2], P('section', None, ('expert', 'dp')), may hold values from 0 to 31, all different within a row; in each aligned block of 128 rows (0 to 127, 128 to 255, ..., all dimensions but the last counted through in order) at most 12 rows name the same one
- router: bfloat16 [2, 1024, 32], P('section'), may hold values from -0.1875 to 0.1875
- w_gate: bfloat16 [2, 32, 1024, 512], P('section', 'expert'), may hold values from -0.1875 to 0.1875
- w_up: bfloat16 [2, 32, 1024, 512], P('section', 'expert'), may hold values from -0.1875 to 0.1875
- w_down: bfloat16 [2, 32, 512, 1024], P('section', 'expert'), may hold values from -0.25 to 0.25
Outputs:
- out_layers: bfloat16 [2, 2, 16384, 1024], P('section', None, ('expert', 'dp'))
- grad_in: bfloat16 [2, 2, 16384, 1024], P('section', None, ('expert', 'dp'))
- grad_gate: float32 [2, 32, 1024, 512], P('section', 'expert', 'dp')
- grad_up: float32 [2, 32, 1024, 512], P('section', 'expert', 'dp')
- grad_down: float32 [2, 32, 512, 1024], P('section', 'expert', 'dp')
- grad_router: float32 [2, 1024, 32], P('section')
Inputs may be any that keep to these rules, and one draw needn't show every extreme that they name: `routes`: each token names 2 different experts. Within the tokens of one device (an aligned block of 128 tokens of one layer and micro-batch) no expert is named by more than 12 tokens, and in every draw some expert is named by exactly 12 tokens of some block.
All inputs are finite; a program needn't handle non-finite values.
Results may differ from a plain program's by a relative error of at most 0.012.
Values may be sent and summed in bfloat16 or wider, within the bound.
No kernel may reach another device: no remote copies, remote signals or barrier semaphores. Data moves between devices by JAX's collectives and lax.ppermute only.
A program may use at most 128 MiB of HBM per device.

v0:
```python
import math
import jax
import jax.numpy as jnp
from jax import lax
from jax.sharding import PartitionSpec as P


def from_behind(array, axis, by):
    length = lax.axis_size(axis)
    pairs = [(i, i + by) for i in range(length) if 0 <= i + by < length]
    return lax.ppermute(array, axis, pairs)


def contract_last(left, right):
    return lax.dot_general(
        left, right, (((1,), (1,)), ((), ())), preferred_element_type=jnp.float32
    )


def contract_first(left, right):
    return lax.dot_general(
        left, right, (((0,), (0,)), ((), ())), preferred_element_type=jnp.float32
    )


def slot_index(chosen, experts, capacity):
    flat = chosen.reshape(-1)
    labels = jnp.arange(experts, dtype=jnp.int32)
    onehot = (flat[:, None] == labels[None, :]).astype(jnp.int32)
    before = jnp.cumsum(onehot, axis=0) - onehot
    position = jnp.sum(before * onehot, axis=1)
    return flat * capacity + position


def route_weights(hidden, chosen, router_layer):
    logits = jnp.dot(hidden, router_layer, preferred_element_type=jnp.float32)
    labels = jnp.arange(logits.shape[1], dtype=jnp.int32)
    match = chosen[:, :, None] == labels[None, None, :]
    picked = jnp.sum(jnp.where(match, logits[:, None, :], 0.0), axis=2)
    raised = jnp.exp(picked)
    return raised / jnp.sum(raised, axis=1, keepdims=True)


def expert_trade(block):
    return lax.all_to_all(block, "expert", split_axis=0, concat_axis=0, tiled=True)


def fetch(store, place):
    return lax.dynamic_index_in_dim(store, place, 0, keepdims=False)


def store_at(store, value, place, valid):
    previous = fetch(store, place)
    return lax.dynamic_update_index_in_dim(store, jnp.where(valid, value, previous), place, 0)


def shards(tokens, cotangent, routes, router, w_gate, w_up, w_down):
    sections = lax.axis_size("section")
    sources = lax.axis_size("expert")
    groups = lax.axis_size("dp")
    section_id = lax.axis_index("section")
    batches, per_device, width = tokens.shape
    top = routes.shape[3]
    experts = router.shape[2]
    capacity = 3 * per_device * top // (2 * experts)
    router_layer = router[0]
    gate_weight = w_gate[0, 0]
    up_weight = w_up[0, 0]
    down_weight = w_down[0, 0]
    units = gate_weight.shape[1]
    total_rows = sources * capacity
    ticks = batches + sections - 1
    chosen_all = routes[0]
    labels = jnp.arange(experts, dtype=jnp.int32)
    kept_inputs = jnp.zeros((batches, per_device, width), jnp.bfloat16)
    kept_picked = jnp.zeros((batches, per_device * top, width), jnp.bfloat16)
    kept_rows = jnp.zeros((batches, total_rows, width), jnp.bfloat16)
    outputs = jnp.zeros((batches, per_device, width), jnp.bfloat16)
    carried = jnp.zeros((per_device, width), jnp.bfloat16)
    for tick in range(ticks):
        batch_index = tick - section_id
        valid = jnp.logical_and(batch_index >= 0, batch_index < batches)
        place = jnp.clip(batch_index, 0, batches - 1)
        fresh = tokens[tick] if tick < batches else jnp.zeros((per_device, width), jnp.bfloat16)
        hidden = jnp.where(section_id == 0, fresh, carried)
        chosen = fetch(chosen_all, place)
        weights = route_weights(hidden, chosen, router_layer)
        index = slot_index(chosen, experts, capacity)
        spread = (
            jnp.zeros((experts * capacity, width), jnp.bfloat16)
            .at[index]
            .set(jnp.repeat(hidden, top, axis=0))
        )
        arrived = expert_trade(spread.reshape(experts, capacity, width)).reshape(total_rows, width)
        gate = jnp.dot(arrived, gate_weight, preferred_element_type=jnp.float32)
        up_term = jnp.dot(arrived, up_weight, preferred_element_type=jnp.float32)
        inner = (jax.nn.silu(gate) * up_term).astype(jnp.bfloat16)
        produced = jnp.dot(inner, down_weight, preferred_element_type=jnp.float32).astype(
            jnp.bfloat16
        )
        returned = expert_trade(produced.reshape(sources, capacity, width)).reshape(
            experts * capacity, width
        )
        picked = returned[index]
        blended = jnp.sum(
            weights[:, :, None] * picked.reshape(per_device, top, width).astype(jnp.float32), axis=1
        )
        mixed = (hidden.astype(jnp.float32) + blended).astype(jnp.bfloat16)
        outputs = store_at(outputs, mixed, place, valid)
        kept_inputs = store_at(kept_inputs, hidden, place, valid)
        kept_picked = store_at(kept_picked, picked, place, valid)
        kept_rows = store_at(kept_rows, arrived, place, valid)
        if tick + 1 < ticks:
            carried = from_behind(mixed, "section", 1)
    kept_dgate = jnp.zeros((batches, total_rows, units), jnp.bfloat16)
    kept_dup = jnp.zeros((batches, total_rows, units), jnp.bfloat16)
    kept_inner = jnp.zeros((batches, total_rows, units), jnp.bfloat16)
    kept_grads = jnp.zeros((batches, total_rows, width), jnp.bfloat16)
    sum_router = jnp.zeros((width, experts), jnp.float32)
    grad_store = jnp.zeros((batches, per_device, width), jnp.bfloat16)
    carried = jnp.zeros((per_device, width), jnp.bfloat16)
    for tick in range(ticks):
        batch_index = tick - (sections - 1 - section_id)
        valid = jnp.logical_and(batch_index >= 0, batch_index < batches)
        place = jnp.clip(batch_index, 0, batches - 1)
        fresh = cotangent[tick] if tick < batches else jnp.zeros((per_device, width), jnp.bfloat16)
        upstream = jnp.where(section_id == sections - 1, fresh, carried)
        upstream = jnp.where(valid, upstream, jnp.zeros_like(upstream))
        chosen = fetch(chosen_all, place)
        hidden = fetch(kept_inputs, place)
        picked = fetch(kept_picked, place)
        arrived = fetch(kept_rows, place)
        weights = route_weights(hidden, chosen, router_layer)
        index = slot_index(chosen, experts, capacity)
        flowing = upstream.astype(jnp.float32)
        along = jnp.sum(
            flowing[:, None, :] * picked.reshape(per_device, top, width).astype(jnp.float32), axis=2
        )
        grad_y = (
            (weights[:, :, None] * flowing[:, None, :])
            .astype(jnp.bfloat16)
            .reshape(per_device * top, width)
        )
        spread = jnp.zeros((experts * capacity, width), jnp.bfloat16).at[index].set(grad_y)
        grad_rows = expert_trade(spread.reshape(experts, capacity, width)).reshape(
            total_rows, width
        )
        gate = jnp.dot(arrived, gate_weight, preferred_element_type=jnp.float32)
        up_term = jnp.dot(arrived, up_weight, preferred_element_type=jnp.float32)
        active = jax.nn.silu(gate)
        inner = (active * up_term).astype(jnp.bfloat16)
        d_hidden = contract_last(grad_rows, down_weight)
        sigma = jax.nn.sigmoid(gate)
        d_gate = (d_hidden * up_term * sigma * (1.0 + gate * (1.0 - sigma))).astype(jnp.bfloat16)
        d_up = (d_hidden * active).astype(jnp.bfloat16)
        d_rows = (contract_last(d_gate, gate_weight) + contract_last(d_up, up_weight)).astype(
            jnp.bfloat16
        )
        returned = expert_trade(d_rows.reshape(sources, capacity, width)).reshape(
            experts * capacity, width
        )
        back = returned[index].reshape(per_device, top, width)
        grad_h = flowing + jnp.sum(back.astype(jnp.float32), axis=1)
        grad_s = weights * (along - jnp.sum(weights * along, axis=1, keepdims=True))
        match = chosen[:, :, None] == labels[None, None, :]
        grad_logits = jnp.sum(jnp.where(match, grad_s[:, :, None], 0.0), axis=1).astype(
            jnp.bfloat16
        )
        local_router = contract_first(hidden, grad_logits)
        grad_h = grad_h + contract_last(grad_logits, router_layer)
        passed = grad_h.astype(jnp.bfloat16)
        grad_store = store_at(grad_store, passed, place, valid)
        kept_dgate = store_at(kept_dgate, d_gate, place, valid)
        kept_dup = store_at(kept_dup, d_up, place, valid)
        kept_inner = store_at(kept_inner, inner, place, valid)
        kept_grads = store_at(kept_grads, grad_rows, place, valid)
        sum_router = sum_router + local_router
        if tick + 1 < ticks:
            carried = from_behind(passed, "section", -1)
    all_rows = kept_rows.reshape(batches * total_rows, width)
    whole_gate = contract_first(all_rows, kept_dgate.reshape(batches * total_rows, units))
    whole_up = contract_first(all_rows, kept_dup.reshape(batches * total_rows, units))
    whole_down = contract_first(
        kept_inner.reshape(batches * total_rows, units),
        kept_grads.reshape(batches * total_rows, width),
    )
    shares = (
        lax.psum_scatter(
            whole_gate.astype(jnp.bfloat16), "dp", scatter_dimension=0, tiled=True
        ).astype(jnp.float32),
        lax.psum_scatter(
            whole_up.astype(jnp.bfloat16), "dp", scatter_dimension=0, tiled=True
        ).astype(jnp.float32),
        lax.psum_scatter(
            whole_down.astype(jnp.bfloat16), "dp", scatter_dimension=0, tiled=True
        ).astype(jnp.float32),
    )
    sum_gate = shares[0]
    sum_up = shares[1]
    sum_down = shares[2]
    sum_router = lax.psum(sum_router, ("expert", "dp"))
    expert_scale = 1.0 / math.sqrt(batches * groups * per_device * top)
    router_scale = 1.0 / math.sqrt(batches * per_device * sources * groups)
    return (
        outputs[None],
        grad_store[None],
        (sum_gate * expert_scale)[None, None],
        (sum_up * expert_scale)[None, None],
        (sum_down * expert_scale)[None, None],
        (sum_router * router_scale)[None],
    )


def solution(mesh):
    placed = (
        P(None, ("expert", "dp"), None),
        P(None, ("expert", "dp"), None),
        P("section", None, ("expert", "dp"), None),
        P("section", None, None),
        P("section", "expert", None, None),
        P("section", "expert", None, None),
        P("section", "expert", None, None),
    )
    return jax.shard_map(
        shards,
        mesh=mesh,
        in_specs=placed,
        out_specs=(
            P("section", None, ("expert", "dp"), None),
            P("section", None, ("expert", "dp"), None),
            P("section", "expert", "dp", None),
            P("section", "expert", "dp", None),
            P("section", "expert", "dp", None),
            P("section", None, None),
        ),
        check_vma=False,
    )
```

profile of v0, /device:TPU:2, one launch (start us, length us, event | category | flops | bytes accessed | tf_op | source)
XLA Modules:
  0.0 838.8 jit_solution(2187735484304862792)
XLA Ops:
  18.5 37.8 %all_to_all.60 = bf16[32,12,1024]{2,1,0:T(8,128)(2,1)S(1)} all-to-all(bf16[32,12,1024]{2,1,0:T(8,128)(2,1)} %reshape.769), channel_id=1, replica_groups=mesh['section'=2,'expert'=32,'dp'=4] {'expert'}, dimensions={0} | all-to-all | bytes 1572864 | tf_op jit(solution)/shard_map/all_to_all | solution.py:45
  61.1 3.4 convolution_convert_fusion.2
  66.7 7.7 all-to-all-start.1
  77.3 22.9 %all-to-all-done.1 = bf16[32,12,1024]{2,1,0:T(8,128)(2,1)} async-done(((bf16[32,12,1024]{2,1,0:T(8,128)(2,1)}), bf16[32,12,1024]{2,1,0:T(8,128)(2,1)}, u32[]{:S(2)}, u32[]{:S(2)}) %all-to-all-start.1) | async-done | bytes 786464 | tf_op jit(solution)/shard_map/all_to_all | solution.py:45
  102.3 3.7 gather_fusion
  106.0 2.7 reshape.804
  122.6 3.1 scatter_custom_fusion.1
  127.9 7.5 all-to-all-start.2
  138.1 23.8 %all-to-all-done.2 = bf16[32,12,1024]{2,1,0:T(8,128)(2,1)} async-done(((bf16[32,12,1024]{2,1,0:T(8,128)(2,1)}), bf16[32,12,1024]{2,1,0:T(8,128)(2,1)}, u32[]{:S(2)}, u32[]{:S(2)}) %all-to-all-start.2) | async-done | bytes 786464 | tf_op jit(solution)/shard_map/all_to_all | solution.py:45
  166.6 3.4 convolution_convert_fusion.1
  172.2 7.8 all-to-all-start.3
  198.5 7.4 all-to-all-done.3
  208.0 3.7 gather_fusion.1
  224.9 3.1 scatter_custom_fusion.2
  230.2 7.5 all-to-all-start.4
  237.7 26.0 %all-to-all-done.4 = bf16[32,12,1024]{2,1,0:T(8,128)(2,1)} async-done(((bf16[32,12,1024]{2,1,0:T(8,128)(2,1)}), bf16[32,12,1024]{2,1,0:T(8,128)(2,1)}, u32[]{:S(2)}, u32[]{:S(2)}) %all-to-all-start.4) | async-done | bytes 786464 | tf_op jit(solution)/shard_map/all_to_all | solution.py:45
  268.5 3.4 convolution_convert_fusion
  274.1 7.6 all-to-all-start.5
  284.1 2.9 mul.359
  287.0 2.9 mul.351
  300.9 6.7 all-to-all-done.5
  309.7 3.6 gather_fusion.2
  322.1 3.4 scatter_custom_fusion.3
  327.6 7.9 all-to-all-start.6
  365.2 3.6 select_bitcast_fusion.1
  373.2 10.0 %all-to-all-start.7 = ((bf16[32,12,1024]{2,1,0:T(8,128)(2,1)}), bf16[32,12,1024]{2,1,0:T(8,128)(2,1)}, u32[]{:S(2)}, u32[]{:S(2)}) async-start(bf16[32,12,1024]{2,1,0:T(8,128)(2,1)} %reshape.790), calls=%async_computation.7 | async-start | bytes 2097152 | tf_op jit(solution)/shard_map/all_to_all | solution.py:45
  398.0 9.3 %all-to-all-done.7 = bf16[32,12,1024]{2,1,0:T(8,128)(2,1)} async-done(((bf16[32,12,1024]{2,1,0:T(8,128)(2,1)}), bf16[32,12,1024]{2,1,0:T(8,128)(2,1)}, u32[]{:S(2)}, u32[]{:S(2)}) %all-to-all-start.7) | async-done | bytes 786464 | tf_op jit(solution)/shard_map/all_to_all | solution.py:45
  409.4 3.7 gather_fusion.3
  415.8 3.3 reduce_sum.337
  426.3 3.0 mul.376
  429.3 2.9 mul.368
  439.0 3.3 scatter_custom_fusion.4
  444.4 7.6 all-to-all-start.8
  481.4 4.0 fusion.94
  489.6 9.5 %all-to-all-start.9 = ((bf16[32,12,1024]{2,1,0:T(8,128)(2,1)}), bf16[32,12,1024]{2,1,0:T(8,128)(2,1)}, u32[]{:S(2)}, u32[]{:S(2)}) async-start(bf16[32,12,1024]{2,1,0:T(8,128)(2,1)} %reshape.795), calls=%async_computation.9 | async-start | bytes 2097152 | tf_op jit(solution)/shard_map/all_to_all | solution.py:45
  511.6 14.2 %all-to-all-done.9 = bf16[32,12,1024]{2,1,0:T(8,128)(2,1)} async-done(((bf16[32,12,1024]{2,1,0:T(8,128)(2,1)}), bf16[32,12,1024]{2,1,0:T(8,128)(2,1)}, u32[]{:S(2)}, u32[]{:S(2)}) %all-to-all-start.9) | async-done | bytes 786464 | tf_op jit(solution)/shard_map/all_to_all | solution.py:45
  527.9 3.7 gather_fusion.4
  534.2 3.3 reduce_sum.346
  549.7 3.0 mul.393
  552.7 2.9 mul.385
  558.8 3.4 scatter_custom_fusion.5
  564.3 7.8 all-to-all-start.10
  601.4 4.2 fusion.93
  614.1 3.4 bitcast_convert_fusion
  621.2 3.7 bitcast_convert_fusion.1
  632.3 9.8 %all-to-all-start.11 = ((bf16[32,12,1024]{2,1,0:T(8,128)(2,1)}), bf16[32,12,1024]{2,1,0:T(8,128)(2,1)}, u32[]{:S(2)}, u32[]{:S(2)}) async-start(bf16[32,12,1024]{2,1,0:T(8,128)(2,1)} %reshape.800), calls=%async_computation.11 | async-start | bytes 2097152 | tf_op jit(solution)/shard_map/all_to_all | solution.py:45
  642.5 3.5 bitcast_convert_fusion.2
  653.2 162.6 %all-reduce.2.cloned.1.call-done = f32[1024,32]{0,1:T(8,128)} async-done(((f32[1024,32]{0,1:T(8,128)}), f32[1024,32]{0,1:T(8,128)}) %all-reduce.2.cloned.1.call-update) | async-done | bytes 131088 | tf_op jit(solution)/shard_map/psum | solution.py:201
  (396 shorter events, 326.2 us)
Async XLA Ops:
  8.0 53.1 %copy-start = (bf16[1,1,512,1024]{3,2,1,0:T(8,128)(2,1)S(1)}, bf16[1,1,512,1024]{3,2,1,0:T(8,128)(2,1)}, u32[]{:S(2)}) copy-start(bf16[1,1,512,1024]{3,2,1,0:T(8,128)(2,1)} %param.13) | copy-start | bytes 3145732
  8.0 5.4 copy-start.20
  9.5 125.8 %copy-start.35 = (s32[1,1,128,2]{2,3,1,0:T(2,128)}, s32[1,1,128,2]{2,3,1,0:T(2,128)S(1)}, u32[]{:S(2)}) copy-start(s32[1,1,128,2]{2,3,1,0:T(2,128)S(1)} %get-tuple-element.57) | copy-start | bytes 3076
  9.5 290.2 %copy-start.32 = (s32[1,1,128,2]{2,3,1,0:T(2,128)}, s32[1,1,128,2]{2,3,1,0:T(2,128)S(1)}, u32[]{:S(2)}) copy-start(s32[1,1,128,2]{2,3,1,0:T(2,128)S(1)} %get-tuple-element.55) | copy-start | bytes 3076
  15.5 40.9 %copy-start.49 = (s32[256,1]{0,1:T(1,128)}, s32[256,1]{0,1:T(1,128)S(1)}, u32[]{:S(2)}) copy-start(s32[256,1]{0,1:T(1,128)S(1)} %get-tuple-element.71) | copy-start | bytes 3076
  18.5 39.9 %copy-start.1 = (bf16[1,1,1024,512]{3,2,1,0:T(8,128)(2,1)S(1)}, bf16[1,1,1024,512]{3,2,1,0:T(8,128)(2,1)}, u32[]{:S(2)}) copy-start(bf16[1,1,1024,512]{3,2,1,0:T(8,128)(2,1)} %param.11) | copy-start | bytes 3145732
  64.5 9.9 %copy-start.11 = (bf16[1,1024,32]{1,2,0:T(8,128)(2,1)S(1)}, bf16[1,1024,32]{1,2,0:T(8,128)(2,1)}, u32[]{:S(2)}) copy-start(bf16[1,1024,32]{1,2,0:T(8,128)(2,1)} %param.10) | copy-start | bytes 196612
  66.7 33.5 %all-to-all-start.1 = ((bf16[32,12,1024]{2,1,0:T(8,128)(2,1)}), bf16[32,12,1024]{2,1,0:T(8,128)(2,1)}, u32[]{:S(2)}, u32[]{:S(2)}) async-start(bf16[32,12,1024]{2,1,0:T(8,128)(2,1)} %reshape.771), calls=%async_computation.1 | async-start | bytes 2097152 | tf_op jit(solution)/shard_map/all_to_all | solution.py:45
  112.9 2.8 collective-permute-start
  127.9 34.1 %all-to-all-start.2 = ((bf16[32,12,1024]{2,1,0:T(8,128)(2,1)}), bf16[32,12,1024]{2,1,0:T(8,128)(2,1)}, u32[]{:S(2)}, u32[]{:S(2)}) async-start(bf16[32,12,1024]{2,1,0:T(8,128)(2,1)} %reshape.775), calls=%async_computation.2 | async-start | bytes 2097152 | tf_op jit(solution)/shard_map/all_to_all | solution.py:45
  172.2 24.4 %copy-start.38 = (s32[1,1,128,2]{2,3,1,0:T(2,128)S(1)}, s32[1,1,128,2]{2,3,1,0:T(2,128)}, u32[]{:S(2)}) copy-start(s32[1,1,128,2]{2,3,1,0:T(2,128)} %copy-done.37) | copy-start | bytes 3076
  172.2 33.7 %all-to-all-start.3 = ((bf16[32,12,1024]{2,1,0:T(8,128)(2,1)}), bf16[32,12,1024]{2,1,0:T(8,128)(2,1)}, u32[]{:S(2)}, u32[]{:S(2)}) async-start(bf16[32,12,1024]{2,1,0:T(8,128)(2,1)} %reshape.777), calls=%async_computation.3 | async-start | bytes 2097152 | tf_op jit(solution)/shard_map/all_to_all | solution.py:45
  214.4 5.0 copy-start.40
  214.4 5.0 copy-start.41
  214.4 5.0 copy-start.47
  214.4 5.0 copy-start.48
  217.9 3.1 collective-permute-start.1
  220.0 4.9 copy-start.46
  230.2 33.6 %all-to-all-start.4 = ((bf16[32,12,1024]{2,1,0:T(8,128)(2,1)}), bf16[32,12,1024]{2,1,0:T(8,128)(2,1)}, u32[]{:S(2)}, u32[]{:S(2)}) async-start(bf16[32,12,1024]{2,1,0:T(8,128)(2,1)} %reshape.781), calls=%async_computation.4 | async-start | bytes 2097152 | tf_op jit(solution)/shard_map/all_to_all | solution.py:45
  274.1 33.5 %all-to-all-start.5 = ((bf16[32,12,1024]{2,1,0:T(8,128)(2,1)}), bf16[32,12,1024]{2,1,0:T(8,128)(2,1)}, u32[]{:S(2)}, u32[]{:S(2)}) async-start(bf16[32,12,1024]{2,1,0:T(8,128)(2,1)} %reshape.783), calls=%async_computation.5 | async-start | bytes 2097152 | tf_op jit(solution)/shard_map/all_to_all | solution.py:45
  292.8 3.8 copy-start.7
  327.6 35.5 %all-to-all-start.6 = ((bf16[32,12,1024]{2,1,0:T(8,128)(2,1)}), bf16[32,12,1024]{2,1,0:T(8,128)(2,1)}, u32[]{:S(2)}, u32[]{:S(2)}) async-start(bf16[32,12,1024]{2,1,0:T(8,128)(2,1)} %reshape.786), calls=%async_computation.6 | async-start | bytes 2097152 | tf_op jit(solution)/shard_map/all_to_all | solution.py:45
  371.0 12.2 %copy-start.39 = (s32[2,128]{1,0:T(2,128)S(1)}, s32[2,128]{1,0:T(2,128)}, u32[]{:S(2)}) copy-start(s32[2,128]{1,0:T(2,128)} %eq.337) | copy-start | bytes 3076
  373.2 19.4 %copy-start.30 = (s32[32,2,128]{2,0,1:T(8,128)S(1)}, s32[32,2,128]{2,0,1:T(8,128)}, u32[]{:S(2)}) copy-start(s32[32,2,128]{2,0,1:T(8,128)} %reduce-window.54) | copy-start | bytes 98308
  373.2 34.1 %all-to-all-start.7 = ((bf16[32,12,1024]{2,1,0:T(8,128)(2,1)}), bf16[32,12,1024]{2,1,0:T(8,128)(2,1)}, u32[]{:S(2)}, u32[]{:S(2)}) async-start(bf16[32,12,1024]{2,1,0:T(8,128)(2,1)} %reshape.790), calls=%async_computation.7 | async-start | bytes 2097152 | tf_op jit(solution)/shard_map/all_to_all | solution.py:45
  394.0 19.1 %copy-start.43 = (s32[256,1]{0,1:T(1,128)}, s32[256,1]{0,1:T(1,128)S(1)}, u32[]{:S(2)}) copy-start(s32[256,1]{0,1:T(1,128)S(1)} %compare_select_fusion.1) | copy-start | bytes 3076
  419.1 5.0 copy-start.23
  420.6 3.5 collective-permute-start.2
  423.4 5.9 copy-start.51
  444.4 34.8 %all-to-all-start.8 = ((bf16[32,12,1024]{2,1,0:T(8,128)(2,1)}), bf16[32,12,1024]{2,1,0:T(8,128)(2,1)}, u32[]{:S(2)}, u32[]{:S(2)}) async-start(bf16[32,12,1024]{2,1,0:T(8,128)(2,1)} %reshape.793), calls=%async_computation.8 | async-start | bytes 2097152 | tf_op jit(solution)/shard_map/all_to_all | solution.py:45
  453.2 45.9 %copy-start.44 = (f32[128,2]{0,1:T(2,128)}, f32[128,2]{0,1:T(2,128)S(1)}, u32[]{:S(2)}) copy-start(f32[128,2]{0,1:T(2,128)S(1)} %select_reduce_fusion.1) | copy-start | bytes 3076
  489.6 36.1 %all-to-all-start.9 = ((bf16[32,12,1024]{2,1,0:T(8,128)(2,1)}), bf16[32,12,1024]{2,1,0:T(8,128)(2,1)}, u32[]{:S(2)}, u32[]{:S(2)}) async-start(bf16[32,12,1024]{2,1,0:T(8,128)(2,1)} %reshape.795), calls=%async_computation.9 | async-start | bytes 2097152 | tf_op jit(solution)/shard_map/all_to_all | solution.py:45
  507.8 3.8 copy-start.34
  507.8 3.8 copy-start.52
  537.5 5.2 copy-start.12
  539.9 7.4 collective-permute-start.3
  552.7 4.7 copy-start.45
  564.3 35.0 %all-to-all-start.10 = ((bf16[32,12,1024]{2,1,0:T(8,128)(2,1)}), bf16[32,12,1024]{2,1,0:T(8,128)(2,1)}, u32[]{:S(2)}, u32[]{:S(2)}) async-start(bf16[32,12,1024]{2,1,0:T(8,128)(2,1)} %reshape.798), calls=%async_computation.10 | async-start | bytes 2097152 | tf_op jit(solution)/shard_map/all_to_all | solution.py:45
  572.1 243.8 %all-reduce.2.cloned.1.call-start = ((), (), s32[]{:S(2)}) async-start(), calls=%async_computation.18 | async-start | bytes 262144 | tf_op jit(solution)/shard_map/psum | solution.py:201
  599.0 226.4 %reduce-scatter.8.cloned.1.call-start = ((), (), s32[]{:S(2)}) async-start(), calls=%async_computation.17 | async-start | bytes 1310720 | tf_op jit(solution)/shard_map/reduce_scatter | solution.py:194
  617.5 209.9 %reduce-scatter.6.cloned.1.call-start = ((), (), s32[]{:S(2)}) async-start(), calls=%async_computation.16 | async-start | bytes 1310720 | tf_op jit(solution)/shard_map/reduce_scatter | solution.py:191
  631.0 11.4 %copy-start.15 = (bf16[2,384,512]{1,2,0:T(8,128)(2,1)S(1)}, bf16[2,384,512]{1,2,0:T(8,128)(2,1)}, u32[]{:S(2)}) copy-start(bf16[2,384,512]{1,2,0:T(8,128)(2,1)} %constant_dynamic-update-slice_fusion.8) | copy-start | bytes 2359300
  631.0 11.4 %copy-start.19 = (bf16[1,384,512]{1,2,0:T(8,128)(2,1)S(1)}, bf16[1,384,512]{1,2,0:T(8,128)(2,1)}, u32[]{:S(2)}) copy-start(bf16[1,384,512]{1,2,0:T(8,128)(2,1)} %copy.133) | copy-start | bytes 1179652
  632.3 185.2 %all-to-all-start.11 = ((bf16[32,12,1024]{2,1,0:T(8,128)(2,1)}), bf16[32,12,1024]{2,1,0:T(8,128)(2,1)}, u32[]{:S(2)}, u32[]{:S(2)}) async-start(bf16[32,12,1024]{2,1,0:T(8,128)(2,1)} %reshape.800), calls=%async_computation.11 | async-start | bytes 2097152 | tf_op jit(solution)/shard_map/all_to_all | solution.py:45
  642.1 187.0 %reduce-scatter.4.cloned.1.call-start = ((), (), s32[]{:S(2)}) async-start(), calls=%async_computation.15 | async-start | bytes 1310720 | tf_op jit(solution)/shard_map/reduce_scatter | solution.py:188
  647.0 4.3 copy-start.25
  652.4 165.0 %copy-start.26 = (bf16[1,2,128,1024]{3,2,1,0:T(8,128)(2,1)}, bf16[1,2,128,1024]{3,2,1,0:T(8,128)(2,1)S(1)}, u32[]{:S(2)}) copy-start(bf16[1,2,128,1024]{3,2,1,0:T(8,128)(2,1)S(1)} %fusion.109) | copy-start | bytes 1572868
  825.3 5.6 copy-start.28
  (25 other events, 53.8 us)
Sparse Core Ops, SparseCore 0:
  599.1 216.7 all-reduce.1
Sparse Core Ops, SparseCore 1:
  617.5 27.5 reduce-scatter.7
  647.6 25.9 reduce-scatter.5
  675.9 26.1 reduce-scatter.3
where the time goes:
time: 853 us; the launch traced here: 839 us
  waiting for transfers between devices  274 us (32%)
  local copies, waits for them, and re-layouts  234 us (27%)
  other arithmetic  102 us (12%)
  starting transfers between devices  97.7 us (11%)
  matrix products  76.8 us (9%)
  blocking collectives  37.8 us (4%)
  between operations  16.9 us (2%)
    psum x1, waiting for transfers between devices, shards(): sum_router = lax.psum(sum_router, ('expert', 'dp'))  163 us
    all_to_all x11, waiting for transfers between devices, expert_trade(): lax.all_to_all(block, 'expert', split_axis=0, concat_axis=0, tiled=True)  111 us
    all_to_all x11, starting transfers between devices, expert_trade(): lax.all_to_all(block, 'expert', split_axis=0, concat_axis=0, tiled=True)  90.7 us
    all_to_all x1, blocking collectives, expert_trade(): lax.all_to_all(block, 'expert', split_axis=0, concat_axis=0, tiled=True)  37.8 us
    dynamic_slice x22, local copies, waits for them, and re-layouts, fetch(): return lax.dynamic_index_in_dim(store, place, 0, keepdims=False)  25.3 us
    dot_general x12, matrix products, contract_last(): lax.dot_general(left, right, (((1,), (1,)), ((), ())), preferred_element_...  23.4 us
    dynamic_update_slice x12, other arithmetic, store_at(): lax.dynamic_update_index_in_dim(store, jnp.where(valid, value, previous),...  22.2 us
    mul x9, local copies, waits for them, and re-layouts, shards(): weights[:, :, None] * flowing[:, None, :]  21.8 us
  transfers between devices with their start and end apart: 19, of which 9 were waited for; matrix products, arithmetic and copies ran while one was open for 26% of the time, Pallas kernels for 0%

commit v1 on v0

--- a/solution.py
+++ b/solution.py
@@ -3,6 +3,10 @@
 import jax.numpy as jnp
 from jax import lax
 from jax.sharding import PartitionSpec as P
+
+
+def number_tables(a0):
+    return lax.all_gather(a0, ("expert", "dp")).sum(axis=0)
 
 
 def from_behind(array, axis, by):
@@ -198,7 +202,7 @@
     sum_gate = shares[0]
     sum_up = shares[1]
     sum_down = shares[2]
-    sum_router = lax.psum(sum_router, ("expert", "dp"))
+    sum_router = number_tables(sum_router)
     expert_scale = 1.0 / math.sqrt(batches * groups * per_device * top)
     router_scale = 1.0 / math.sqrt(batches * per_device * sources * groups)
     return (

time: 853 us -> 843 us (0.988)
  waiting for transfers between devices: 274 us -> 231 us
  blocking collectives: 37.8 us -> 71.4 us
  starting transfers between devices: 97.7 us -> 86.3 us
    psum x1 -> x0, waiting for transfers between devices: 163 us -> none  [shards(): sum_router = lax.psum(sum_router, ('expert', 'dp'))]
    all_gather x0 -> x1, waiting for transfers between devices: none -> 102 us  [number_tables(): return lax.all_gather(a0, ('expert', 'dp')).sum(axis=0)]
    all_to_all x1 -> x2, blocking collectives: 37.8 us -> 71.4 us  [expert_trade(): lax.all_to_all(block, 'expert', split_axis=0, concat_axis=0, tiled=True)]
    all_to_all x11 -> x10, waiting for transfers between devices: 111 us -> 129 us  [expert_trade(): lax.all_to_all(block, 'expert', split_axis=0, concat_axis=0, tiled=True)]
    unnamed x110 -> x99, local copies, waits for them, and re-layouts: 10 us -> 26.5 us
    all_to_all x11 -> x10, starting transfers between devices: 90.7 us -> 80 us  [expert_trade(): lax.all_to_all(block, 'expert', split_axis=0, concat_axis=0, tiled=True)]
  transfers between devices with their start and end apart: 19 -> 18, of which waited for: 9 -> 13; matrix products, arithmetic and copies ran while one was open for 26% -> 23% of each run, Pallas kernels for 0% -> 0%
where the time goes in v1:
time: 843 us; the launch traced here: 828 us
  local copies, waits for them, and re-layouts  242 us (29%)
  waiting for transfers between devices  231 us (27%)
  other arithmetic  106 us (13%)
  starting transfers between devices  86.3 us (10%)
  matrix products  74.5 us (9%)
  blocking collectives  71.4 us (8%)
  between operations  16.4 us (2%)
    all_to_all x10, waiting for transfers between devices, expert_trade(): lax.all_to_all(block, 'expert', split_axis=0, concat_axis=0, tiled=True)  129 us
    all_gather x1, waiting for transfers between devices, number_tables(): return lax.all_gather(a0, ('expert', 'dp')).sum(axis=0)  102 us
    all_to_all x10, starting transfers between devices, expert_trade(): lax.all_to_all(block, 'expert', split_axis=0, concat_axis=0, tiled=True)  80 us
    all_to_all x2, blocking collectives, expert_trade(): lax.all_to_all(block, 'expert', split_axis=0, concat_axis=0, tiled=True)  71.4 us
    unnamed x99, local copies, waits for them, and re-layouts  26.5 us
    dynamic_slice x22, local copies, waits for them, and re-layouts, fetch(): return lax.dynamic_index_in_dim(store, place, 0, keepdims=False)  25.3 us
    dynamic_update_slice x12, other arithmetic, store_at(): lax.dynamic_update_index_in_dim(store, jnp.where(valid, value, previous),...  22.3 us
    dot_general x12, matrix products, contract_last(): lax.dot_general(left, right, (((1,), (1,)), ((), ())), preferred_element_...  22.2 us
  transfers between devices with their start and end apart: 18, of which 13 were waited for; matrix products, arithmetic and copies ran while one was open for 23% of the time, Pallas kernels for 0%

profile of v1, /device:TPU:2, one launch (start us, length us, event | category | flops | bytes accessed | tf_op | source)
XLA Modules:
  0.0 828.1 jit_solution(5291505058692671329)
XLA Ops:
  18.6 37.8 %all_to_all.60 = bf16[32,12,1024]{2,1,0:T(8,128)(2,1)S(1)} all-to-all(bf16[32,12,1024]{2,1,0:T(8,128)(2,1)} %reshape.778), channel_id=1, replica_groups=mesh['section'=2,'expert'=32,'dp'=4] {'expert'}, dimensions={0} | all-to-all | bytes 1572864 | tf_op jit(solution)/shard_map/all_to_all | solution.py:49
  61.2 3.4 convolution_convert_fusion.2
  66.7 7.7 all-to-all-start.1
  77.3 22.9 %all-to-all-done.1 = bf16[32,12,1024]{2,1,0:T(8,128)(2,1)} async-done(((bf16[32,12,1024]{2,1,0:T(8,128)(2,1)}), bf16[32,12,1024]{2,1,0:T(8,128)(2,1)}, u32[]{:S(2)}, u32[]{:S(2)}) %all-to-all-start.1) | async-done | bytes 786464 | tf_op jit(solution)/shard_map/all_to_all | solution.py:49
  102.4 3.7 gather_fusion
  122.5 3.1 scatter_custom_fusion.1
  127.9 7.5 all-to-all-start.2
  139.3 22.7 %all-to-all-done.2 = bf16[32,12,1024]{2,1,0:T(8,128)(2,1)} async-done(((bf16[32,12,1024]{2,1,0:T(8,128)(2,1)}), bf16[32,12,1024]{2,1,0:T(8,128)(2,1)}, u32[]{:S(2)}, u32[]{:S(2)}) %all-to-all-start.2) | async-done | bytes 786464 | tf_op jit(solution)/shard_map/all_to_all | solution.py:49
  166.7 3.4 convolution_convert_fusion.1
  172.3 7.7 all-to-all-start.3
  195.7 10.3 %all-to-all-done.3 = bf16[32,12,1024]{2,1,0:T(8,128)(2,1)} async-done(((bf16[32,12,1024]{2,1,0:T(8,128)(2,1)}), bf16[32,12,1024]{2,1,0:T(8,128)(2,1)}, u32[]{:S(2)}, u32[]{:S(2)}) %all-to-all-start.3) | async-done | bytes 786464 | tf_op jit(solution)/shard_map/all_to_all | solution.py:49
  208.0 3.6 gather_fusion.1
  224.9 3.1 scatter_custom_fusion.2
  230.2 33.6 %all_to_all.61 = bf16[32,12,1024]{2,1,0:T(8,128)(2,1)} all-to-all(bf16[32,12,1024]{2,1,0:T(8,128)(2,1)} %reshape.790), channel_id=1, replica_groups=mesh['section'=2,'expert'=32,'dp'=4] {'expert'}, dimensions={0} | all-to-all | bytes 1572864 | tf_op jit(solution)/shard_map/all_to_all | solution.py:49
  268.5 3.4 convolution_convert_fusion
  274.0 7.6 all-to-all-start.5
  284.1 3.0 mul.369
  287.0 3.0 mul.361
  297.0 10.5 %all-to-all-done.5 = bf16[32,12,1024]{2,1,0:T(8,128)(2,1)} async-done(((bf16[32,12,1024]{2,1,0:T(8,128)(2,1)}), bf16[32,12,1024]{2,1,0:T(8,128)(2,1)}, u32[]{:S(2)}, u32[]{:S(2)}) %all-to-all-start.5) | async-done | bytes 786464 | tf_op jit(solution)/shard_map/all_to_all | solution.py:49
  309.6 3.6 gather_fusion.2
  319.1 3.3 scatter_custom_fusion.3
  324.6 8.1 all-to-all-start.6
  353.6 4.7 all-to-all-done.6
  360.4 3.6 select_bitcast_fusion.1
  368.2 7.4 all-to-all-start.7
  384.1 17.4 %all-to-all-done.7 = bf16[32,12,1024]{2,1,0:T(8,128)(2,1)} async-done(((bf16[32,12,1024]{2,1,0:T(8,128)(2,1)}), bf16[32,12,1024]{2,1,0:T(8,128)(2,1)}, u32[]{:S(2)}, u32[]{:S(2)}) %all-to-all-start.7) | async-done | bytes 786464 | tf_op jit(solution)/shard_map/all_to_all | solution.py:49
  403.6 3.6 gather_fusion.3
  409.9 3.3 reduce_sum.346
  420.2 3.0 mul.386
  423.2 2.9 mul.378
  431.1 3.4 scatter_custom_fusion.4
  436.6 7.5 all-to-all-start.8
  473.2 4.0 fusion.94
  481.5 8.6 %all-to-all-start.9 = ((bf16[32,12,1024]{2,1,0:T(8,128)(2,1)}), bf16[32,12,1024]{2,1,0:T(8,128)(2,1)}, u32[]{:S(2)}, u32[]{:S(2)}) async-start(bf16[32,12,1024]{2,1,0:T(8,128)(2,1)} %reshape.804), calls=%async_computation.9 | async-start | bytes 2097152 | tf_op jit(solution)/shard_map/all_to_all | solution.py:49
  499.1 17.5 %all-to-all-done.9 = bf16[32,12,1024]{2,1,0:T(8,128)(2,1)} async-done(((bf16[32,12,1024]{2,1,0:T(8,128)(2,1)}), bf16[32,12,1024]{2,1,0:T(8,128)(2,1)}, u32[]{:S(2)}, u32[]{:S(2)}) %all-to-all-start.9) | async-done | bytes 786464 | tf_op jit(solution)/shard_map/all_to_all | solution.py:49
  518.7 3.6 gather_fusion.4
  525.0 3.3 reduce_sum.355
  548.6 3.3 scatter_custom_fusion.5
  554.1 7.6 all-to-all-start.10
  591.8 4.3 fusion.93
  599.8 3.6 bitcast_convert_fusion.2
  607.2 3.7 bitcast_convert_fusion.1
  629.6 3.4 bitcast_convert_fusion
  640.6 10.3 %all-to-all-start.11 = ((bf16[32,12,1024]{2,1,0:T(8,128)(2,1)}), bf16[32,12,1024]{2,1,0:T(8,128)(2,1)}, u32[]{:S(2)}, u32[]{:S(2)}) async-start(bf16[32,12,1024]{2,1,0:T(8,128)(2,1)} %reshape.809), calls=%async_computation.11 | async-start | bytes 2097152 | tf_op jit(solution)/shard_map/all_to_all | solution.py:49
  658.7 21.3 %all-to-all-done.11 = bf16[32,12,1024]{2,1,0:T(8,128)(2,1)} async-done(((bf16[32,12,1024]{2,1,0:T(8,128)(2,1)}), bf16[32,12,1024]{2,1,0:T(8,128)(2,1)}, u32[]{:S(2)}, u32[]{:S(2)}) %all-to-all-start.11) | async-done | bytes 786464 | tf_op jit(solution)/shard_map/all_to_all | solution.py:49
  692.6 101.8 %all-gather.3.cloned.1.call-done = f32[131072,32]{0,1:T(8,128)} async-done(((f32[1024,32]{0,1:T(8,128)}), f32[131072,32]{0,1:T(8,128)}) %all-gather.3.cloned.1.call-update) | async-done | bytes 16777232 | tf_op jit(solution)/shard_map/all_gather | solution.py:9
  794.3 17.7 %copy.158 = f32[4,8,128,1024]{3,2,1,0:T(8,128)} copy(f32[4,8,128,1024]{3,1,2,0:T(8,128)} %bitcast.446) | data formatting | bytes 33554432
  812.0 8.1 bitcast_reduce_fusion
  (385 shorter events, 320.1 us)
Async XLA Ops:
  8.0 53.2 %copy-start = (bf16[1,1,512,1024]{3,2,1,0:T(8,128)(2,1)S(1)}, bf16[1,1,512,1024]{3,2,1,0:T(8,128)(2,1)}, u32[]{:S(2)}) copy-start(bf16[1,1,512,1024]{3,2,1,0:T(8,128)(2,1)} %param.13) | copy-start | bytes 3145732
  8.0 5.4 copy-start.18
  9.5 3.0 copy-start.37
  9.5 172.6 %copy-start.35 = (s32[1,1,128,2]{2,3,1,0:T(2,128)}, s32[1,1,128,2]{2,3,1,0:T(2,128)S(1)}, u32[]{:S(2)}) copy-start(s32[1,1,128,2]{2,3,1,0:T(2,128)S(1)} %get-tuple-element.57) | copy-start | bytes 3076
  9.6 286.8 %copy-start.32 = (s32[1,1,128,2]{2,3,1,0:T(2,128)}, s32[1,1,128,2]{2,3,1,0:T(2,128)S(1)}, u32[]{:S(2)}) copy-start(s32[1,1,128,2]{2,3,1,0:T(2,128)S(1)} %get-tuple-element.55) | copy-start | bytes 3076
  9.6 407.7 %copy-start.31 = (s32[1,1,128,2]{2,3,1,0:T(2,128)}, s32[1,1,128,2]{2,3,1,0:T(2,128)S(1)}, u32[]{:S(2)}) copy-start(s32[1,1,128,2]{2,3,1,0:T(2,128)S(1)} %get-tuple-element.63) | copy-start | bytes 3076
  9.6 480.5 %copy-start.28 = (s32[1,1,128,2]{2,3,1,0:T(2,128)}, s32[1,1,128,2]{2,3,1,0:T(2,128)S(1)}, u32[]{:S(2)}) copy-start(s32[1,1,128,2]{2,3,1,0:T(2,128)S(1)} %get-tuple-element.21) | copy-start | bytes 3076
  15.5 40.9 %copy-start.43 = (s32[256,1]{0,1:T(1,128)}, s32[256,1]{0,1:T(1,128)S(1)}, u32[]{:S(2)}) copy-start(s32[256,1]{0,1:T(1,128)S(1)} %get-tuple-element.71) | copy-start | bytes 3076
  18.6 39.9 %copy-start.1 = (bf16[1,1,1024,512]{3,2,1,0:T(8,128)(2,1)S(1)}, bf16[1,1,1024,512]{3,2,1,0:T(8,128)(2,1)}, u32[]{:S(2)}) copy-start(bf16[1,1,1024,512]{3,2,1,0:T(8,128)(2,1)} %param.11) | copy-start | bytes 3145732
  58.5 2.7 copy-start.2
  64.6 9.8 %copy-start.11 = (bf16[1,1024,32]{1,2,0:T(8,128)(2,1)S(1)}, bf16[1,1024,32]{1,2,0:T(8,128)(2,1)}, u32[]{:S(2)}) copy-start(bf16[1,1024,32]{1,2,0:T(8,128)(2,1)} %param.10) | copy-start | bytes 196612
  66.7 33.5 %all-to-all-start.1 = ((bf16[32,12,1024]{2,1,0:T(8,128)(2,1)}), bf16[32,12,1024]{2,1,0:T(8,128)(2,1)}, u32[]{:S(2)}, u32[]{:S(2)}) async-start(bf16[32,12,1024]{2,1,0:T(8,128)(2,1)} %reshape.780), calls=%async_computation.1 | async-start | bytes 2097152 | tf_op jit(solution)/shard_map/all_to_all | solution.py:49
  113.0 2.6 collective-permute-start
  127.9 34.2 %all-to-all-start.2 = ((bf16[32,12,1024]{2,1,0:T(8,128)(2,1)}), bf16[32,12,1024]{2,1,0:T(8,128)(2,1)}, u32[]{:S(2)}, u32[]{:S(2)}) async-start(bf16[32,12,1024]{2,1,0:T(8,128)(2,1)} %reshape.784), calls=%async_computation.2 | async-start | bytes 2097152 | tf_op jit(solution)/shard_map/all_to_all | solution.py:49
  172.3 33.7 %all-to-all-start.3 = ((bf16[32,12,1024]{2,1,0:T(8,128)(2,1)}), bf16[32,12,1024]{2,1,0:T(8,128)(2,1)}, u32[]{:S(2)}, u32[]{:S(2)}) async-start(bf16[32,12,1024]{2,1,0:T(8,128)(2,1)} %reshape.786), calls=%async_computation.3 | async-start | bytes 2097152 | tf_op jit(solution)/shard_map/all_to_all | solution.py:49
  214.3 2.7 copy-start.19
  214.3 5.0 copy-start.38
  214.3 5.1 copy-start.39
  214.3 5.1 copy-start.41
  214.4 5.1 copy-start.42
  217.9 3.1 collective-permute-start.1
  274.0 33.5 %all-to-all-start.5 = ((bf16[32,12,1024]{2,1,0:T(8,128)(2,1)}), bf16[32,12,1024]{2,1,0:T(8,128)(2,1)}, u32[]{:S(2)}, u32[]{:S(2)}) async-start(bf16[32,12,1024]{2,1,0:T(8,128)(2,1)} %reshape.792), calls=%async_computation.5 | async-start | bytes 2097152 | tf_op jit(solution)/shard_map/all_to_all | solution.py:49
  290.0 3.2 copy-start.7
  296.4 16.7 %copy-start.44 = (f32[128,2]{0,1:T(2,128)}, f32[128,2]{0,1:T(2,128)S(1)}, u32[]{:S(2)}) copy-start(f32[128,2]{0,1:T(2,128)S(1)} %select_reduce_fusion.5) | copy-start | bytes 3076
  324.6 33.7 %all-to-all-start.6 = ((bf16[32,12,1024]{2,1,0:T(8,128)(2,1)}), bf16[32,12,1024]{2,1,0:T(8,128)(2,1)}, u32[]{:S(2)}, u32[]{:S(2)}) async-start(bf16[32,12,1024]{2,1,0:T(8,128)(2,1)} %reshape.795), calls=%async_computation.6 | async-start | bytes 2097152 | tf_op jit(solution)/shard_map/all_to_all | solution.py:49
  368.2 33.3 %all-to-all-start.7 = ((bf16[32,12,1024]{2,1,0:T(8,128)(2,1)}), bf16[32,12,1024]{2,1,0:T(8,128)(2,1)}, u32[]{:S(2)}, u32[]{:S(2)}) async-start(bf16[32,12,1024]{2,1,0:T(8,128)(2,1)} %reshape.799), calls=%async_computation.7 | async-start | bytes 2097152 | tf_op jit(solution)/shard_map/all_to_all | solution.py:49
  413.1 4.9 copy-start.22
  414.6 3.3 copy-start.8
  414.6 3.4 collective-permute-start.2
  417.3 5.9 copy-start.46
  436.6 34.5 %all-to-all-start.8 = ((bf16[32,12,1024]{2,1,0:T(8,128)(2,1)}), bf16[32,12,1024]{2,1,0:T(8,128)(2,1)}, u32[]{:S(2)}, u32[]{:S(2)}) async-start(bf16[32,12,1024]{2,1,0:T(8,128)(2,1)} %reshape.802), calls=%async_computation.8 | async-start | bytes 2097152 | tf_op jit(solution)/shard_map/all_to_all | solution.py:49
  481.5 35.1 %all-to-all-start.9 = ((bf16[32,12,1024]{2,1,0:T(8,128)(2,1)}), bf16[32,12,1024]{2,1,0:T(8,128)(2,1)}, u32[]{:S(2)}, u32[]{:S(2)}) async-start(bf16[32,12,1024]{2,1,0:T(8,128)(2,1)} %reshape.804), calls=%async_computation.9 | async-start | bytes 2097152 | tf_op jit(solution)/shard_map/all_to_all | solution.py:49
  525.0 7.9 copy-start.29
  530.5 3.4 collective-permute-start.3
  533.0 6.0 copy-start.45
  554.1 35.6 %all-to-all-start.10 = ((bf16[32,12,1024]{2,1,0:T(8,128)(2,1)}), bf16[32,12,1024]{2,1,0:T(8,128)(2,1)}, u32[]{:S(2)}, u32[]{:S(2)}) async-start(bf16[32,12,1024]{2,1,0:T(8,128)(2,1)} %reshape.807), calls=%async_computation.10 | async-start | bytes 2097152 | tf_op jit(solution)/shard_map/all_to_all | solution.py:49
  561.8 125.2 %reduce-scatter.4.cloned.1.call-start = ((), (), s32[]{:S(2)}) async-start(), calls=%async_computation.15 | async-start | bytes 1310720 | tf_op jit(solution)/shard_map/reduce_scatter | solution.py:192
  603.5 85.5 %reduce-scatter.6.cloned.1.call-start = ((), (), s32[]{:S(2)}) async-start(), calls=%async_computation.16 | async-start | bytes 1310720 | tf_op jit(solution)/shard_map/reduce_scatter | solution.py:195
  610.9 79.8 %reduce-scatter.8.cloned.1.call-start = ((), (), s32[]{:S(2)}) async-start(), calls=%async_computation.17 | async-start | bytes 1310720 | tf_op jit(solution)/shard_map/reduce_scatter | solution.py:198
  633.0 161.3 %all-gather.3.cloned.1.call-start = ((), (), s32[]{:S(2)}) async-start(), calls=%async_computation.18 | async-start | bytes 16908288 | tf_op jit(solution)/shard_map/all_gather | solution.py:9
  639.4 11.5 %copy-start.40 = (s32[256,1]{0,1:T(1,128)S(1)}, s32[256,1]{0,1:T(1,128)}, u32[]{:S(2)}) copy-start(s32[256,1]{0,1:T(1,128)} %compare_select_fusion) | copy-start | bytes 3076
  640.6 11.6 %copy-start.36 = (s32[1,1,128,2]{2,3,1,0:T(2,128)S(1)}, s32[1,1,128,2]{2,3,1,0:T(2,128)}, u32[]{:S(2)}) copy-start(s32[1,1,128,2]{2,3,1,0:T(2,128)} %copy-done.35) | copy-start | bytes 3076
  640.6 11.8 %copy-start.6 = (bf16[256,1024]{1,0:T(8,128)(2,1)S(1)}, bf16[256,1024]{1,0:T(8,128)(2,1)}, u32[]{:S(2)}) copy-start(bf16[256,1024]{1,0:T(8,128)(2,1)} %gather_fusion.2) | copy-start | bytes 1572868
  640.6 39.3 %all-to-all-start.11 = ((bf16[32,12,1024]{2,1,0:T(8,128)(2,1)}), bf16[32,12,1024]{2,1,0:T(8,128)(2,1)}, u32[]{:S(2)}, u32[]{:S(2)}) async-start(bf16[32,12,1024]{2,1,0:T(8,128)(2,1)} %reshape.809), calls=%async_computation.11 | async-start | bytes 2097152 | tf_op jit(solution)/shard_map/all_to_all | solution.py:49
  654.1 3.7 copy-start.9
  657.8 22.2 %copy-start.25 = (bf16[1,2,128,1024]{3,2,1,0:T(8,128)(2,1)}, bf16[1,2,128,1024]{3,2,1,0:T(8,128)(2,1)S(1)}, u32[]{:S(2)}) copy-start(bf16[1,2,128,1024]{3,2,1,0:T(8,128)(2,1)S(1)} %fusion.109) | copy-start | bytes 1572868
  682.5 4.2 copy-start.21
  686.9 125.1 %copy-start.24 = (bf16[1,2,128,1024]{3,2,1,0:T(8,128)(2,1)}, bf16[1,2,128,1024]{3,2,1,0:T(8,128)(2,1)S(1)}, u32[]{:S(2)}) copy-start(bf16[1,2,128,1024]{3,2,1,0:T(8,128)(2,1)S(1)} %fusion.112) | copy-start | bytes 1572868
  (18 other events, 28.0 us)
Sparse Core Ops, SparseCore 0:
  603.6 27.3 reduce-scatter.3
  633.6 26.0 reduce-scatter.5
  662.2 26.0 reduce-scatter.7
Sparse Core Ops, SparseCore 1:
  637.7 156.6 all-gather.2
